TPU v7x, 256 devices: a whole 4x4x8 slice. The times are simulated.
256 devices in a mesh: grp: 32 (over z, x), tp: 8 (over y, core).
Axes of the slice: x: 4, y: 4, z: 8, core: 2. Of those that a mesh axis runs over, the one named last changes fastest.
Arguments:
- tokens: bfloat16 [32768, 2048], P('grp'), may hold values from -6 to 6
- norm_gain: float32 [2048], replicated, may hold values from 0.5 to 7
- w_qkv: bfloat16 [2048, 3, 2048], P(None, None, 'tp'), may hold values from -0.125 to 0.125
- w_out: bfloat16 [2048, 2048], P('tp'), may hold values from -0.125 to 0.125
- a_in: bfloat16 [64, 2048, 48], P('grp', 'tp'), may hold values from -0.125 to 0.125
- b_in: bfloat16 [64, 3, 16, 2048], P('grp', None, None, 'tp'), may hold values from -1.5 to 1.5
- a_out: bfloat16 [64, 2048, 16], P('grp', 'tp'), may hold values from -0.125 to 0.125
- b_out: bfloat16 [64, 16, 2048], P('grp', None, 'tp'), may hold values from -1.5 to 1.5
- req_len: int32 [32, 4], replicated, may hold values from 1 to 512, 1024 in all within a row
- req_adapter: int32 [32, 4], replicated, may hold values from 0 to 63, as said below
- holder: int32 [64], replicated, may hold values from 0 to 63, each once
- page_table: int32 [32, 8], P('grp'), may hold values from 0 to 7, each once within a row
Outputs:
- layer_out: bfloat16 [32768, 2048], P('grp', 'tp')
- kv_pages: bfloat16 [256, 2, 128, 2048], P('grp', None, None, 'tp')
Inputs may be any that keep to these rules, and one draw needn't show every extreme that they name: `req_adapter`: exactly 16 different adapters appear among all requests.
All inputs are finite; a program needn't handle non-finite values.
Results may differ from a plain program's by a relative error of at most 0.017.
The roundings to bfloat16 on the way count: a program that leaves them out, or rounds other values in their place, can miss the bound.
Values may be sent and summed in bfloat16 or wider, within the bound.
No kernel may reach another device: no remote copies, remote signals or barrier semaphores. Data moves between devices by JAX's collectives and lax.ppermute only.
A program may use at most 128 MiB of HBM per device.

v0:
```python
import math
import jax
import jax.numpy as jnp
from jax import lax
from jax.sharding import PartitionSpec as P

HD = 128
PAGE = 128
EPSILON = 1e-05
THETA = 10000.0


def shifted(block, axis, distance):
    devices = range(lax.axis_size(axis))
    route = [(i - distance, i) for i in devices if i - distance in devices]
    return lax.ppermute(block, axis, route)


def rms_norm(token_rows, norm_gain):
    values = token_rows.astype(jnp.float32)
    norm_scale = lax.rsqrt(jnp.mean(values * values, axis=-1, keepdims=True) + EPSILON)
    return (values * norm_scale * norm_gain).astype(jnp.bfloat16)


def request_layout(lengths, offset, tok_count):
    end_at = jnp.cumsum(lengths)
    starts = end_at - lengths
    row_ids = jnp.arange(tok_count, dtype=jnp.int32)
    segment = jnp.sum((row_ids[:, None] >= end_at[None, :]).astype(jnp.int32), axis=1)
    member = segment[:, None] == jnp.arange(lengths.shape[0], dtype=jnp.int32)[None, :]
    begin_at = jnp.sum(jnp.where(member, starts[None, :], 0), axis=1)
    position = row_ids - begin_at + jnp.where(segment == 0, offset, 0)
    return (segment, member, position)


def rotate(head_rows, position, head_dim):
    half_dim = head_dim // 2
    frequency = THETA ** (-(jnp.arange(half_dim, dtype=jnp.float32) * (2.0 / head_dim)))
    angles = position.astype(jnp.float32)[:, None] * frequency[None, :]
    cosine = jnp.cos(angles)[:, None, :]
    sine_part = jnp.sin(angles)[:, None, :]
    lower_half = head_rows[..., :half_dim]
    upper_half = head_rows[..., half_dim:]
    return jnp.concatenate(
        [
            lower_half * cosine - upper_half * sine_part,
            upper_half * cosine + lower_half * sine_part,
        ],
        axis=-1,
    )


def local(
    tokens,
    norm_gain,
    w_qkv,
    w_out,
    a_in,
    b_in,
    a_out,
    b_out,
    req_len,
    req_adapter,
    holder,
    page_table,
):
    tok_count = tokens.shape[0]
    local_width = w_out.shape[0]
    local_heads = local_width // HD
    req_count = req_len.shape[1]
    rank_dim = a_out.shape[2]
    group_id = lax.axis_index("grp")
    tp_id = lax.axis_index("tp")
    lengths = lax.dynamic_index_in_dim(req_len, group_id, 0, keepdims=False)
    earlier = lax.dynamic_index_in_dim(req_len, jnp.maximum(group_id - 1, 0), 0, keepdims=False)
    continued = group_id > 0
    prev_len = earlier[req_count - 1]
    offset = jnp.where(continued, prev_len, 0)
    segment, member, position = request_layout(lengths, offset, tok_count)
    wanted = lax.dynamic_index_in_dim(req_adapter, group_id, 0, keepdims=False)
    stacks = (
        lax.all_gather(a_in, "grp", axis=0, tiled=True),
        lax.all_gather(b_in, "grp", axis=0, tiled=True),
        lax.all_gather(a_out, "grp", axis=0, tiled=True),
        lax.all_gather(b_out, "grp", axis=0, tiled=True),
    )
    req_slots = holder[wanted]
    sel_in = jnp.take(stacks[0], req_slots, axis=0)
    sel_up = jnp.take(stacks[1], req_slots, axis=0)
    sel_odown = jnp.take(stacks[2], req_slots, axis=0)
    sel_oup = jnp.take(stacks[3], req_slots, axis=0)
    member_f = member.astype(jnp.float32)
    pick_bf = member.astype(jnp.bfloat16)
    normed = rms_norm(tokens, norm_gain)
    own_cols = lax.dynamic_slice_in_dim(normed, tp_id * local_width, local_width, 1)
    down_f = jnp.einsum("td,rdk->trk", own_cols, sel_in, preferred_element_type=jnp.float32)
    lowrank_f = lax.psum(jnp.sum(down_f * member_f[:, :, None], axis=1), "tp")
    lowrank = lowrank_f.astype(jnp.bfloat16)
    spread = (pick_bf[:, :, None] * lowrank[:, None, :]).reshape(tok_count, req_count, 3, rank_dim)
    delta_qkv = jnp.einsum("trck,rckd->tcd", spread, sel_up, preferred_element_type=jnp.float32)
    base_qkv = jnp.dot(
        normed, w_qkv.reshape(w_qkv.shape[0], 3 * local_width), preferred_element_type=jnp.float32
    )
    qkv = (base_qkv.reshape(tok_count, 3, local_width) + delta_qkv).reshape(
        tok_count, 3, local_heads, HD
    )
    query_rows = rotate(qkv[:, 0], position, HD).astype(jnp.bfloat16)
    key_rows = rotate(qkv[:, 1], position, HD).astype(jnp.bfloat16).reshape(tok_count, local_width)
    value_rows = qkv[:, 2].astype(jnp.bfloat16).reshape(tok_count, local_width)
    row_ids = jnp.arange(tok_count, dtype=jnp.int32)
    far_key, far_value = shifted((key_rows, value_rows), "grp", 1)
    far_ok = continued & (segment[:, None] == 0) & (row_ids[None, :] >= tok_count - prev_len)
    far_count = far_key.shape[0]
    near_ok = (segment[:, None] == segment[None, :]) & (row_ids[None, :] <= row_ids[:, None])
    allowed = jnp.concatenate([far_ok, near_ok], axis=1)
    key_all = jnp.concatenate([far_key, key_rows], axis=0).reshape(
        far_count + tok_count, local_heads, HD
    )
    value_all = jnp.concatenate([far_value, value_rows], axis=0).reshape(
        far_count + tok_count, local_heads, HD
    )
    score_scale = 1.0 / math.sqrt(HD)
    scores = (
        jnp.einsum("thd,shd->hts", query_rows, key_all, preferred_element_type=jnp.float32)
        * score_scale
    )
    scores = jnp.where(allowed[None], scores, -jnp.inf)
    row_top = jnp.max(scores, axis=-1, keepdims=True)
    weights = jnp.exp(scores - row_top)
    weights_bf = (weights / jnp.sum(weights, axis=-1, keepdims=True)).astype(jnp.bfloat16)
    mixed_heads = jnp.einsum(
        "hts,shd->thd", weights_bf, value_all, preferred_element_type=jnp.float32
    )
    attended = mixed_heads.astype(jnp.bfloat16).reshape(tok_count, local_width)
    partial_value = jnp.dot(attended, w_out, preferred_element_type=jnp.float32)
    base_out = lax.psum_scatter(
        partial_value.astype(jnp.bfloat16), "tp", scatter_dimension=1, tiled=True
    ).astype(jnp.float32)
    down_o = jnp.einsum("td,rdk->trk", attended, sel_odown, preferred_element_type=jnp.float32)
    low_o = lax.psum(jnp.sum(down_o * member_f[:, :, None], axis=1).astype(jnp.bfloat16), "tp")
    spread_o = (pick_bf[:, :, None] * low_o[:, None, :]).reshape(tok_count, req_count * rank_dim)
    delta_o = jnp.dot(
        spread_o,
        sel_oup.reshape(req_count * rank_dim, local_width),
        preferred_element_type=jnp.float32,
    )
    own_rows = lax.dynamic_slice_in_dim(tokens, tp_id * local_width, local_width, 1).astype(
        jnp.float32
    )
    layer_out = (own_rows + base_out + delta_o).astype(jnp.bfloat16)
    page_row = page_table[0]
    page_count = page_row.shape[0]
    numbers = jnp.arange(page_count, dtype=jnp.int32)
    inverse = jnp.sum(jnp.where(page_row[:, None] == numbers[None, :], numbers[:, None], 0), axis=0)
    both_blocks = jnp.stack(
        [
            key_rows.reshape(page_count, PAGE, local_width),
            value_rows.reshape(page_count, PAGE, local_width),
        ],
        axis=1,
    )
    kv_pages = jnp.take(both_blocks, inverse, axis=0)
    return (layer_out, kv_pages)


def solution(mesh):
    return jax.shard_map(
        local,
        mesh=mesh,
        in_specs=(
            P("grp", None),
            P(),
            P(None, None, "tp"),
            P("tp", None),
            P("grp", "tp", None),
            P("grp", None, None, "tp"),
            P("grp", "tp", None),
            P("grp", None, "tp"),
            P(),
            P(),
            P(),
            P("grp", None),
        ),
        out_specs=(P("grp", "tp"), P("grp", None, None, "tp")),
        check_vma=False,
    )
```

profile of v0, /device:TPU:2, one launch (start us, length us, event | category | flops | bytes accessed | tf_op | source)
XLA Modules:
  0.0 358.6 jit_solution(400273009174848627)
XLA Ops:
  9.7 1.3 gather_fusion
  13.9 3.1 fusion.2
  17.6 4.7 %copy.40 = bf16[2048,3,256]{0,2,1:T(8,128)(2,1)} copy(bf16[2048,3,256]{2,0,1:T(8,128)(2,1)} %param.14) | data formatting | bytes 6291456 | tf_op args[2]
  22.3 3.0 multiply_cosine_fusion
  25.3 1.5 pad_add_fusion
  27.9 1.9 copy-done.3
  29.8 5.1 %fusion.9 = f32[1024,3,256]{0,2,1:T(8,128)} fusion(bf16[1024,2048]{1,0:T(8,128)(2,1)S(1)} %fusion.4, bf16[2048,3,256]{0,2,1:T(8,128)(2,1)S(1)} %copy-done.5), kind=kOutput, calls=%fused_computation.21 | convolution fusion | flops 3221225472 | bytes 10485760 | tf_op jit(solution)/shard_map/dot_general | solution.py:101
  34.9 54.5 %all-gather.5.cloned.1.call-done = bf16[64,256,48]{1,2,0:T(8,128)(2,1)} async-done(((bf16[2,256,48]{1,2,0:T(8,128)(2,1)}), bf16[64,256,48]{1,2,0:T(8,128)(2,1)}) %all-gather.5.cloned.1.call-update) | async-done | bytes 1572880 | tf_op jit(solution)/shard_map/all_gather | solution.py:82
  89.4 2.0 gather_fusion.2
  91.4 1.4 fusion.22
  92.9 25.7 %all-reduce.1 = bf16[1024,48]{0,1:T(8,128)(2,1)S(1)} all-reduce(f32[1024,48]{0,1:T(8,128)S(1)} %multiply_reduce_fusion), channel_id=1, replica_groups=mesh['grp'=32,'tp'=8] {'tp'}, use_global_device_ids=true, to_apply=%region_4.5 | all-reduce | flops 49152 | bytes 294912 | tf_op jit(solution)/shard_map/psum | solution.py:97
  118.6 47.8 %all-gather.3.cloned.1.call-done = bf16[64,3,16,256]{3,2,1,0:T(8,128)(2,1)} async-done(((bf16[2,3,16,256]{3,2,1,0:T(8,128)(2,1)}), bf16[64,3,16,256]{3,2,1,0:T(8,128)(2,1)}) %all-gather.3.cloned.1.call-update) | async-done | bytes 1572880 | tf_op jit(solution)/shard_map/all_gather | solution.py:83
  166.4 2.0 gather_fusion.1
  168.4 2.6 bitcast_add_fusion
  172.8 1.2 fusion.52
  174.3 3.5 collective-permute-start
  177.8 1.6 copy.55
  179.3 1.6 multiply_subtract_fusion
  182.3 3.2 collective-permute-start.1
  185.5 1.3 slice_bitcast_fusion
  186.8 2.6 subtract_convert_fusion
  189.4 7.9 %collective-permute-done.1 = bf16[1024,256]{0,1:T(8,128)(2,1)} collective-permute-done((bf16[1024,256]{0,1:T(8,128)(2,1)}, bf16[1024,256]{0,1:T(8,128)(2,1)}, u32[]{:S(2)}, u32[]{:S(2)}) %collective-permute-start.1) | collective-permute-done | bytes 524320 | tf_op jit(solution)/shard_map/ppermute | solution.py:16
  197.3 1.3 copy.45
  198.6 10.8 %fusion.53 = (f32[2,1024]{1,0:T(2,128)S(1)}, f32[2,1024,2048]{2,1,0:T(8,128)}) fusion(pred[1024,2048]{1,0:T(8,128)(4,1)} %pad_add_fusion, bf16[1024,2,128]{2,0,1:T(8,128)(2,1)S(1)} %maximum_convert_fusion, bf16[1024,2,128]{2,0,1:T(8,128)(2,1)S(1)} %copy.45, bf16[1024,2,64]{2,0,1:T(8,128)(2,1)} %get-tuple-element.7, bf16[1024,2,64]{2,0,1:T(8,128)(2,1)} %get-tuple-element.6), kind=kOutput, calls=%fused_computation.109 | convolution fusion | flops 1093666816 | bytes 20455424 | tf_op jit(solution)/shard_map/sub | solution.py:129
  209.3 8.9 %fusion.17 = bf16[2,128,1024]{2,1,0:T(8,128)(2,1)S(1)} fusion(f32[2,1024,2048]{2,1,0:T(8,128)} %get-tuple-element.17, f32[2,1024]{1,0:T(2,128)S(1)} %get-tuple-element.16, bf16[1024,2,128]{0,2,1:T(8,128)(2,1)S(1)} %slice_bitcast_fusion, bf16[1024,2,128]{0,2,1:T(8,128)(2,1)} %bitcast.17), kind=kOutput, calls=%fused_computation.33 | convolution fusion | flops 1084489728 | bytes 18358272 | tf_op jit(solution)/shard_map/hts,shd->thd/dot_general | solution.py:131
  219.1 3.2 convolution_convert_fusion
  222.4 49.4 %all_gather.14 = bf16[64,256,16]{1,2,0:T(8,128)(2,1)S(1)} all-gather(bf16[2,256,16]{1,2,0:T(8,128)(2,1)S(1)} %copy-done.7), channel_id=1, replica_groups=mesh['grp'=32,'tp'=8] {'grp'}, dimensions={0}, use_global_device_ids=true | all-gather | bytes 540672 | tf_op jit(solution)/shard_map/all_gather | solution.py:84
  272.4 48.5 %all_gather.15 = bf16[64,16,256]{2,1,0:T(8,128)(2,1)S(1)} all-gather(bf16[2,16,256]{2,1,0:T(8,128)(2,1)S(1)} %copy-done.8), channel_id=1, replica_groups=mesh['grp'=32,'tp'=8] {'grp'}, dimensions={0}, use_global_device_ids=true | all-gather | bytes 540672 | tf_op jit(solution)/shard_map/all_gather | solution.py:85
  323.7 1.1 broadcast_select_fusion
  324.8 1.2 fusion.54
  326.1 23.6 %psum.15 = bf16[1024,16]{0,1:T(8,128)(2,1)S(1)} all-reduce(bf16[1024,16]{0,1:T(8,128)(2,1)S(1)} %multiply_reduce_fusion.1), channel_id=1, replica_groups=mesh['grp'=32,'tp'=8] {'tp'}, use_global_device_ids=true, to_apply=%region_10.11 | all-reduce | flops 16384 | bytes 65536 | tf_op jit(solution)/shard_map/psum | solution.py:140
  349.7 2.3 fusion.16
  (70 shorter events, 13.4 us)
Async XLA Ops:
  7.2 211.9 %copy-start = (bf16[256,2048]{1,0:T(8,128)(2,1)S(1)}, bf16[256,2048]{1,0:T(8,128)(2,1)}, u32[]{:S(2)}) copy-start(bf16[256,2048]{1,0:T(8,128)(2,1)} %param.15) | copy-start | bytes 3145732
  7.2 82.2 %all-gather.5.cloned.1.call-start = ((), (), s32[]{:S(2)}) async-start(), calls=%async_computation.2 | async-start | bytes 1622016 | tf_op jit(solution)/shard_map/all_gather | solution.py:82
  7.9 158.5 %all-gather.3.cloned.1.call-start = ((), (), s32[]{:S(2)}) async-start(), calls=%async_computation.1 | async-start | bytes 1622016 | tf_op jit(solution)/shard_map/all_gather | solution.py:83
  8.7 341.0 %reduce-scatter.2.cloned.1.call-start = ((), (), s32[]{:S(2)}) async-start(), calls=%async_computation.3 | async-start | bytes 4718592 | tf_op jit(solution)/shard_map/reduce_scatter | solution.py:136
  22.3 4.6 %copy-start.9 = (f32[2048]{0:T(1024)S(1)}, f32[2048]{0:T(1024)}, u32[]{:S(2)}) copy-start(f32[2048]{0:T(1024)} %param.13) | copy-start | bytes 24580
  22.3 4.6 %copy-start.1 = (bf16[1024,2048]{1,0:T(8,128)(2,1)S(1)}, bf16[1024,2048]{1,0:T(8,128)(2,1)}, u32[]{:S(2)}) copy-start(bf16[1024,2048]{1,0:T(8,128)(2,1)} %param.12) | copy-start | bytes 12582916
  26.8 3.0 copy-start.5
  27.9 1.9 copy-start.3
  171.0 1.8 copy-start.2
  174.3 35.1 %collective-permute-start = (bf16[1024,256]{0,1:T(8,128)(2,1)}, bf16[1024,256]{0,1:T(8,128)(2,1)}, u32[]{:S(2)}, u32[]{:S(2)}) collective-permute-start(bf16[1024,256]{0,1:T(8,128)(2,1)} %bitcast.83), channel_id=1, source_target_pairs={{0,8},{8,16},{16,24},{24,32},{32,40},{40,48},{48,56},{56,64},{64,7... | collective-permute-start | bytes 1572872 | tf_op jit(solution)/shard_map/ppermute | solution.py:16
  182.3 14.9 %collective-permute-start.1 = (bf16[1024,256]{0,1:T(8,128)(2,1)}, bf16[1024,256]{0,1:T(8,128)(2,1)}, u32[]{:S(2)}, u32[]{:S(2)}) collective-permute-start(bf16[1024,256]{0,1:T(8,128)(2,1)} %bitcast.24), channel_id=1, source_target_pairs={{0,8},{8,16},{16,24},{24,32},{32,40},{40,48},{48,56},{56,64},{64,7... | collective-permute-start | bytes 1572872 | tf_op jit(solution)/shard_map/ppermute | solution.py:16
  218.3 0.8 copy-start.4
  219.1 3.3 copy-start.7
  222.3 50.0 %copy-start.8 = (bf16[2,16,256]{2,1,0:T(8,128)(2,1)S(1)}, bf16[2,16,256]{2,1,0:T(8,128)(2,1)}, u32[]{:S(2)}) copy-start(bf16[2,16,256]{2,1,0:T(8,128)(2,1)} %param.19) | copy-start | bytes 49156
  222.3 99.1 %copy-start.10 = (s32[1,8]{1,0:T(1,128)S(1)}, s32[1,8]{1,0:T(1,128)}, u32[]{:S(2)}) copy-start(s32[1,8]{1,0:T(1,128)} %param.23) | copy-start | bytes 100
  222.3 99.8 %copy-start.6 = (bf16[1024,1,2,128]{0,3,2,1:T(8,128)(2,1)S(1)}, bf16[1024,1,2,128]{0,3,2,1:T(8,128)(2,1)}, u32[]{:S(2)}) copy-start(bf16[1024,1,2,128]{0,3,2,1:T(8,128)(2,1)} %slice.61) | copy-start | bytes 1572868
Sparse Core Ops, SparseCore 0:
  10.6 78.7 all-gather.4
  92.0 74.4 all-gather.2
  222.5 41.1 reduce-scatter.1
where the time goes:
time: 359 us
  blocking collectives  147 us (41%)
  waiting for transfers between devices  112 us (31%)
  matrix products  35.6 us (10%)
  local copies, waits for them, and re-layouts  25.7 us (7%)
  other arithmetic  16.4 us (5%)
  between operations  15.4 us (4%)
  starting transfers between devices  6.77 us (2%)
    all_gather x1, waiting for transfers between devices, local(): lax.all_gather(a_in, 'grp', axis=0, tiled=True)  54.5 us
    all_gather x1, blocking collectives, local(): lax.all_gather(a_out, 'grp', axis=0, tiled=True)  49.4 us
    all_gather x1, blocking collectives, local(): lax.all_gather(b_out, 'grp', axis=0, tiled=True)  48.5 us
    all_gather x1, waiting for transfers between devices, local(): lax.all_gather(b_in, 'grp', axis=0, tiled=True)  47.8 us
    psum x1, blocking collectives, local(): lowrank_f = lax.psum(jnp.sum(down_f * member_f[:, :, None], axis=1), 'tp')  25.7 us
    psum x1, blocking collectives, local(): lax.psum(jnp.sum(down_o * member_f[:, :, None], axis=1).astype(jnp.bfloat...  23.6 us
    sub x1, matrix products, local(): weights = jnp.exp(scores - row_top)  10.8 us
    unnamed x27, local copies, waits for them, and re-layouts  10.4 us
  transfers between devices with their start and end apart: 5, of which 3 were waited for; matrix products, arithmetic and copies ran while one was open for 15% of the time, Pallas kernels for 0%

commit v1 on v0

--- a/solution.py
+++ b/solution.py
@@ -1,3 +1,4 @@
+import functools
 import math
 import jax
 import jax.numpy as jnp
@@ -8,6 +9,16 @@
 PAGE = 128
 EPSILON = 1e-05
 THETA = 10000.0
+
+
+def place_sizes(piece_in, out_dim):
+    gallery = []
+    for _ in range(lax.axis_size("grp")):
+        gallery.append(piece_in)
+    return jnp.concatenate(lax.all_to_all(jnp.stack(gallery), "grp", 0, 0), axis=out_dim)
+
+
+spread_the_group = functools.partial(place_sizes, out_dim=0)
 
 
 def shifted(block, axis, distance):
@@ -81,7 +92,7 @@
     stacks = (
         lax.all_gather(a_in, "grp", axis=0, tiled=True),
         lax.all_gather(b_in, "grp", axis=0, tiled=True),
-        lax.all_gather(a_out, "grp", axis=0, tiled=True),
+        spread_the_group(a_out),
         lax.all_gather(b_out, "grp", axis=0, tiled=True),
     )
     req_slots = holder[wanted]

time: 359 us -> 329 us (0.916)
  blocking collectives: 147 us -> 105 us
  starting transfers between devices: 6.77 us -> 16.1 us
    all_gather x1 -> x0, blocking collectives: 49.4 us -> none  [local(): lax.all_gather(a_out, 'grp', axis=0, tiled=True)]
    all_to_all x0 -> x1, starting transfers between devices: none -> 9.31 us  [place_sizes(): lax.all_to_all(jnp.stack(gallery), 'grp', 0, 0)]
    all_gather x1, blocking collectives: 48.5 us -> 55.7 us  [local(): lax.all_gather(b_out, 'grp', axis=0, tiled=True)]
  transfers between devices with their start and end apart: 5 -> 6, of which waited for: 3 -> 3; matrix products, arithmetic and copies ran while one was open for 15% -> 17% of each run, Pallas kernels for 0% -> 0%
where the time goes in v1:
time: 329 us; the launch traced here: 328 us
  waiting for transfers between devices  112 us (34%)
  blocking collectives  105 us (32%)
  matrix products  35.6 us (11%)
  local copies, waits for them, and re-layouts  27.6 us (8%)
  other arithmetic  16.4 us (5%)
  starting transfers between devices  16.1 us (5%)
  between operations  15.4 us (5%)
    all_gather x1, blocking collectives, local(): lax.all_gather(b_out, 'grp', axis=0, tiled=True)  55.7 us
    all_gather x1, waiting for transfers between devices, local(): lax.all_gather(a_in, 'grp', axis=0, tiled=True)  54.5 us
    all_gather x1, waiting for transfers between devices, local(): lax.all_gather(b_in, 'grp', axis=0, tiled=True)  47.8 us
    psum x1, blocking collectives, local(): lowrank_f = lax.psum(jnp.sum(down_f * member_f[:, :, None], axis=1), 'tp')  25.7 us
    psum x1, blocking collectives, local(): lax.psum(jnp.sum(down_o * member_f[:, :, None], axis=1).astype(jnp.bfloat...  23.6 us
    sub x1, matrix products, local(): weights = jnp.exp(scores - row_top)  10.8 us
    unnamed x27, local copies, waits for them, and re-layouts  10.4 us
    all_to_all x1, starting transfers between devices, place_sizes(): lax.all_to_all(jnp.stack(gallery), 'grp', 0, 0)  9.31 us
  transfers between devices with their start and end apart: 6, of which 3 were waited for; matrix products, arithmetic and copies ran while one was open for 17% of the time, Pallas kernels for 0%

profile of v1, /device:TPU:2, one launch (start us, length us, event | category | flops | bytes accessed | tf_op | source)
XLA Modules:
  0.0 327.6 jit_solution(14673971827651407381)
XLA Ops:
  9.7 1.3 gather_fusion
  13.9 3.1 fusion.2
  17.6 4.7 %copy.42 = bf16[2048,3,256]{0,2,1:T(8,128)(2,1)} copy(bf16[2048,3,256]{2,0,1:T(8,128)(2,1)} %param.14) | data formatting | bytes 6291456 | tf_op args[2]
  22.3 3.0 multiply_cosine_fusion
  25.3 1.5 pad_add_fusion
  27.9 1.9 copy-done.3
  29.8 5.1 %fusion.9 = f32[1024,3,256]{0,2,1:T(8,128)} fusion(bf16[1024,2048]{1,0:T(8,128)(2,1)S(1)} %fusion.4, bf16[2048,3,256]{0,2,1:T(8,128)(2,1)S(1)} %copy-done.5), kind=kOutput, calls=%fused_computation.21 | convolution fusion | flops 3221225472 | bytes 10485760 | tf_op jit(solution)/shard_map/dot_general | solution.py:112
  34.9 54.5 %all-gather.5.cloned.1.call-done = bf16[64,256,48]{1,2,0:T(8,128)(2,1)} async-done(((bf16[2,256,48]{1,2,0:T(8,128)(2,1)}), bf16[64,256,48]{1,2,0:T(8,128)(2,1)}) %all-gather.5.cloned.1.call-update) | async-done | bytes 1572880 | tf_op jit(solution)/shard_map/all_gather | solution.py:93
  89.4 2.0 gather_fusion.2
  91.4 1.4 fusion.22
  92.9 25.7 %all-reduce.1 = bf16[1024,48]{0,1:T(8,128)(2,1)S(1)} all-reduce(f32[1024,48]{0,1:T(8,128)S(1)} %multiply_reduce_fusion), channel_id=1, replica_groups=mesh['grp'=32,'tp'=8] {'tp'}, use_global_device_ids=true, to_apply=%region_4.5 | all-reduce | flops 49152 | bytes 294912 | tf_op jit(solution)/shard_map/psum | solution.py:108
  118.6 47.8 %all-gather.3.cloned.1.call-done = bf16[64,3,16,256]{3,2,1,0:T(8,128)(2,1)} async-done(((bf16[2,3,16,256]{3,2,1,0:T(8,128)(2,1)}), bf16[64,3,16,256]{3,2,1,0:T(8,128)(2,1)}) %all-gather.3.cloned.1.call-update) | async-done | bytes 1572880 | tf_op jit(solution)/shard_map/all_gather | solution.py:94
  166.4 2.0 gather_fusion.1
  168.4 2.6 bitcast_add_fusion
  172.8 1.2 fusion.52
  174.3 3.5 %collective-permute-start = (bf16[1024,256]{0,1:T(8,128)(2,1)}, bf16[1024,256]{0,1:T(8,128)(2,1)}, u32[]{:S(2)}, u32[]{:S(2)}) collective-permute-start(bf16[1024,256]{0,1:T(8,128)(2,1)} %bitcast.84), channel_id=1, source_target_pairs={{0,8},{8,16},{16,24},{24,32},{32,40},{40,48},{48,56},{56,64},{64,7... | collective-permute-start | bytes 1572872 | tf_op jit(solution)/shard_map/ppermute | solution.py:27
  177.8 1.6 copy.57
  179.3 1.6 multiply_subtract_fusion
  182.3 3.2 collective-permute-start.1
  185.5 1.3 slice_bitcast_fusion
  186.8 2.6 subtract_convert_fusion
  189.4 7.9 %collective-permute-done.1 = bf16[1024,256]{0,1:T(8,128)(2,1)} collective-permute-done((bf16[1024,256]{0,1:T(8,128)(2,1)}, bf16[1024,256]{0,1:T(8,128)(2,1)}, u32[]{:S(2)}, u32[]{:S(2)}) %collective-permute-start.1) | collective-permute-done | bytes 524320 | tf_op jit(solution)/shard_map/ppermute | solution.py:27
  197.3 1.3 copy.47
  198.6 10.8 %fusion.53 = (f32[2,1024]{1,0:T(2,128)S(1)}, f32[2,1024,2048]{2,1,0:T(8,128)}) fusion(pred[1024,2048]{1,0:T(8,128)(4,1)} %pad_add_fusion, bf16[1024,2,128]{2,0,1:T(8,128)(2,1)S(1)} %maximum_convert_fusion, bf16[1024,2,128]{2,0,1:T(8,128)(2,1)S(1)} %copy.47, bf16[1024,2,64]{2,0,1:T(8,128)(2,1)} %get-tuple-element.7, bf16[1024,2,64]{2,0,1:T(8,128)(2,1)} %get-tuple-element.6), kind=kOutput, calls=%fused_computation.109 | convolution fusion | flops 1093666816 | bytes 20455424 | tf_op jit(solution)/shard_map/sub | solution.py:140
  209.3 8.9 %fusion.17 = bf16[2,128,1024]{2,1,0:T(8,128)(2,1)S(1)} fusion(f32[2,1024,2048]{2,1,0:T(8,128)} %get-tuple-element.17, f32[2,1024]{1,0:T(2,128)S(1)} %get-tuple-element.16, bf16[1024,2,128]{0,2,1:T(8,128)(2,1)S(1)} %slice_bitcast_fusion, bf16[1024,2,128]{0,2,1:T(8,128)(2,1)} %bitcast.17), kind=kOutput, calls=%fused_computation.33 | convolution fusion | flops 1084489728 | bytes 18358272 | tf_op jit(solution)/shard_map/hts,shd->thd/dot_general | solution.py:142
  219.1 3.2 convolution_convert_fusion
  223.2 9.3 %all-to-all-start = ((bf16[32,2,256,16]{2,3,1,0:T(8,128)(2,1)}), bf16[32,2,256,16]{2,3,1,0:T(8,128)(2,1)S(1)}, u32[]{:S(2)}, u32[]{:S(2)}) async-start(bf16[32,2,256,16]{2,3,1,0:T(8,128)(2,1)} %stack.4), calls=%async_computation.1 | async-start | bytes 1048576 | tf_op jit(solution)/shard_map/all_to_all | solution.py:18
  232.6 55.7 %all_gather.11 = bf16[64,16,256]{2,1,0:T(8,128)(2,1)} all-gather(bf16[2,16,256]{2,1,0:T(8,128)(2,1)S(1)} %copy-done.8), channel_id=1, replica_groups=mesh['grp'=32,'tp'=8] {'grp'}, dimensions={0}, use_global_device_ids=true | all-gather | bytes 540672 | tf_op jit(solution)/shard_map/all_gather | solution.py:96
  288.3 1.6 gather_fusion.4
  293.9 1.2 fusion.54
  295.1 23.6 %psum.15 = bf16[1024,16]{0,1:T(8,128)(2,1)S(1)} all-reduce(bf16[1024,16]{0,1:T(8,128)(2,1)S(1)} %multiply_reduce_fusion.1), channel_id=1, replica_groups=mesh['grp'=32,'tp'=8] {'tp'}, use_global_device_ids=true, to_apply=%region_10.11 | all-reduce | flops 16384 | bytes 65536 | tf_op jit(solution)/shard_map/psum | solution.py:151
  318.8 2.3 fusion.16
  (72 shorter events, 14.8 us)
Async XLA Ops:
  7.2 211.9 %copy-start = (bf16[256,2048]{1,0:T(8,128)(2,1)S(1)}, bf16[256,2048]{1,0:T(8,128)(2,1)}, u32[]{:S(2)}) copy-start(bf16[256,2048]{1,0:T(8,128)(2,1)} %param.15) | copy-start | bytes 3145732
  7.2 82.2 %all-gather.5.cloned.1.call-start = ((), (), s32[]{:S(2)}) async-start(), calls=%async_computation.3 | async-start | bytes 1622016 | tf_op jit(solution)/shard_map/all_gather | solution.py:93
  7.9 158.5 %all-gather.3.cloned.1.call-start = ((), (), s32[]{:S(2)}) async-start(), calls=%async_computation.2 | async-start | bytes 1622016 | tf_op jit(solution)/shard_map/all_gather | solution.py:94
  8.7 310.1 %reduce-scatter.2.cloned.1.call-start = ((), (), s32[]{:S(2)}) async-start(), calls=%async_computation.4 | async-start | bytes 4718592 | tf_op jit(solution)/shard_map/reduce_scatter | solution.py:147
  22.3 4.6 %copy-start.9 = (f32[2048]{0:T(1024)S(1)}, f32[2048]{0:T(1024)}, u32[]{:S(2)}) copy-start(f32[2048]{0:T(1024)} %param.13) | copy-start | bytes 24580
  22.3 4.6 %copy-start.1 = (bf16[1024,2048]{1,0:T(8,128)(2,1)S(1)}, bf16[1024,2048]{1,0:T(8,128)(2,1)}, u32[]{:S(2)}) copy-start(bf16[1024,2048]{1,0:T(8,128)(2,1)} %param.12) | copy-start | bytes 12582916
  26.8 3.0 copy-start.5
  27.9 1.9 copy-start.3
  171.0 1.8 copy-start.2
  174.3 35.1 %collective-permute-start = (bf16[1024,256]{0,1:T(8,128)(2,1)}, bf16[1024,256]{0,1:T(8,128)(2,1)}, u32[]{:S(2)}, u32[]{:S(2)}) collective-permute-start(bf16[1024,256]{0,1:T(8,128)(2,1)} %bitcast.84), channel_id=1, source_target_pairs={{0,8},{8,16},{16,24},{24,32},{32,40},{40,48},{48,56},{56,64},{64,7... | collective-permute-start | bytes 1572872 | tf_op jit(solution)/shard_map/ppermute | solution.py:27
  182.3 14.9 %collective-permute-start.1 = (bf16[1024,256]{0,1:T(8,128)(2,1)}, bf16[1024,256]{0,1:T(8,128)(2,1)}, u32[]{:S(2)}, u32[]{:S(2)}) collective-permute-start(bf16[1024,256]{0,1:T(8,128)(2,1)} %bitcast.24), channel_id=1, source_target_pairs={{0,8},{8,16},{16,24},{24,32},{32,40},{40,48},{48,56},{56,64},{64,7... | collective-permute-start | bytes 1572872 | tf_op jit(solution)/shard_map/ppermute | solution.py:27
  218.3 0.8 copy-start.4
  219.1 3.3 copy-start.7
  222.3 10.2 %copy-start.8 = (bf16[2,16,256]{2,1,0:T(8,128)(2,1)S(1)}, bf16[2,16,256]{2,1,0:T(8,128)(2,1)}, u32[]{:S(2)}) copy-start(bf16[2,16,256]{2,1,0:T(8,128)(2,1)} %param.19) | copy-start | bytes 49156
  222.3 67.6 %copy-start.10 = (s32[1,8]{1,0:T(1,128)S(1)}, s32[1,8]{1,0:T(1,128)}, u32[]{:S(2)}) copy-start(s32[1,8]{1,0:T(1,128)} %param.23) | copy-start | bytes 100
  222.4 68.9 %copy-start.6 = (bf16[1024,1,2,128]{0,3,2,1:T(8,128)(2,1)S(1)}, bf16[1024,1,2,128]{0,3,2,1:T(8,128)(2,1)}, u32[]{:S(2)}) copy-start(bf16[1024,1,2,128]{0,3,2,1:T(8,128)(2,1)} %slice.61) | copy-start | bytes 1572868
  223.2 66.8 %all-to-all-start = ((bf16[32,2,256,16]{2,3,1,0:T(8,128)(2,1)}), bf16[32,2,256,16]{2,3,1,0:T(8,128)(2,1)S(1)}, u32[]{:S(2)}, u32[]{:S(2)}) async-start(bf16[32,2,256,16]{2,3,1,0:T(8,128)(2,1)} %stack.4), calls=%async_computation.1 | async-start | bytes 1048576 | tf_op jit(solution)/shard_map/all_to_all | solution.py:18
Sparse Core Ops, SparseCore 0:
  10.6 78.7 all-gather.4
  92.0 74.4 all-gather.2
  222.5 41.2 reduce-scatter.1
